TPU v7x, 128 devices: a whole 4x4x4 slice. The times are simulated.
128 devices in a mesh: dp: 4 (over z_hi, core), mp: 32 (over x, y, z_lo).
Axes of the slice: x: 4, y: 4, z: 4 (z_hi: 2, z_lo: 2; z = z_hi * 2 + z_lo), core: 2. Of those that a mesh axis runs over, the one named last changes fastest.
Arguments:
- residual_input: bfloat16 [2048, 4608], P(('dp', 'mp')), may hold values from -6 to 6
- before_attention_gain: float32 [4608], replicated, may hold values from 0.25 to 1.75
- after_attention_gain: float32 [4608], replicated, may hold values from 0.25 to 1.75
- before_feedforward_gain: float32 [4608], replicated, may hold values from 0.25 to 1.75
- after_feedforward_gain: float32 [4608], replicated, may hold values from 0.25 to 1.75
- query_weight: bfloat16 [4608, 4096], P(None, 'mp'), may hold values from -0.09375 to 0.09375
- key_value_weight: bfloat16 [4608, 2, 32, 128], P(None, None, 'mp'), as said below
- output_weight: bfloat16 [4096, 4608], P('mp'), may hold values from -0.09375 to 0.09375
- gate_matrix: bfloat16 [4608, 20480], P(None, 'mp'), may hold values from -0.09375 to 0.09375
- up_matrix: bfloat16 [4608, 20480], P(None, 'mp'), may hold values from -0.09375 to 0.09375
- down_matrix: bfloat16 [20480, 4608], P('mp'), may hold values from -0.0390625 to 0.0390625
- key_value_cache: bfloat16 [256, 2, 32, 16, 128], P('dp', None, 'mp'), as said below
- projected_lowrank_left: bfloat16 [64, 4608, 16], P('mp'), may hold values from -0.09375 to 0.09375
- projected_lowrank_right: bfloat16 [64, 16, 3, 32, 128], P(None, None, None, 'mp'), as said below
- result_lowrank_left: bfloat16 [64, 4096, 16], P(None, 'mp'), may hold values from -0.09375 to 0.09375
- result_lowrank_right: bfloat16 [64, 16, 4608], P('mp'), may hold values from -1.5 to 1.5
- token_request: int32 [4, 512], P('dp'), may hold values from 0 to 7, never falling along the last dimension, each value on 1 to 256 neighbouring positions
- lowrank_choice_by_prompt: int32 [4, 8], P('dp'), may hold values from 0 to 63
- adapter_position: int32 [64], replicated, may hold values from 0 to 63, each once
- request_pages: int32 [4, 8, 4], replicated, may hold values from 0 to 255
Outputs:
- hidden_out: bfloat16 [2048, 4608], P(('dp', 'mp'))
- kv_new: bfloat16 [2048, 2, 32, 128], P('dp', None, 'mp')
Inputs may be any that keep to these rules, and one draw needn't show every extreme that they name: `key_value_weight`: query heads h and h2 with h // 2 == h2 // 2 have equal key and value weights: they share one key and value head. `key_value_cache`: query heads that share a key and value head have equal cached keys and values. `projected_lowrank_right`: the key and value parts of query heads that share a key and value head are equal. `token_request`: numbers never fall along a group; every request has at least one token. `adapter_position`: each slot once. `request_pages`: pages may repeat within and across requests.
All inputs are finite; a program needn't handle non-finite values.
Results may differ from a plain program's by a relative error of at most 0.035.
Values may be sent and summed in bfloat16 or wider, within the bound.
No kernel may reach another device: no remote copies, remote signals or barrier semaphores. Data moves between devices by JAX's collectives and lax.ppermute only.
A program may use at most 128 MiB of HBM per device.

v0:
```python
import math
import jax
import jax.numpy as jnp
from jax import lax
from jax.sharding import PartitionSpec as P

HIDDEN_BREADTH = 4608
ASKING_CHANNELS = 32
CHANNEL_LENGTH = 128
NUM_LOW_TERMS = 64
LOW_DIMENSION = 16
SHARD_PROMPTS = 8
PPR = 4
PAGE = 16
EPS = 1e-06
SOFTCAP = 50.0
DP_AXES = ("zh", "c")
MP_AXES = ("x", "y", "zl")
MP_STAGES = (("zl",), ("x", "y"))


def gather_mp(values):
    for stage in MP_STAGES:
        values = lax.all_gather(values, stage, axis=0, tiled=True)
    return values


def scatter_mp(values):
    for stage in reversed(MP_STAGES):
        values = lax.psum_scatter(values, stage, scatter_dimension=0, tiled=True)
    return values


def sum_mp(values):
    for stage in MP_STAGES:
        values = lax.psum(values, stage)
    return values


def rms_scale(values, scaling):
    mean_square = jnp.mean(values * values, axis=-1, keepdims=True)
    return values * lax.rsqrt(mean_square + EPS) * scaling


def apply_rotary(values, token_positions):
    half_dim = values.shape[-1] // 2
    frequency = 10000.0 ** (-2.0 * jnp.arange(half_dim, dtype=jnp.float32) / values.shape[-1])
    angles = token_positions.astype(jnp.float32)[:, None] * frequency[None, :]
    cosine = jnp.cos(angles)[:, None, :]
    sine_part = jnp.sin(angles)[:, None, :]
    first_half = values[..., :half_dim]
    second_half = values[..., half_dim:]
    return jnp.concatenate(
        [
            first_half * cosine - second_half * sine_part,
            second_half * cosine + first_half * sine_part,
        ],
        axis=-1,
    )


def positions_of(segments):
    length = segments.shape[0]
    earlier = jnp.sum((segments[None, :] < segments[:, None]).astype(jnp.int32), axis=1)
    return PPR * PAGE + jnp.arange(length, dtype=jnp.int32) - earlier


def capped(scores):
    return SOFTCAP * jnp.tanh(scores / SOFTCAP)


def attend_local(query_rows, keys_new, fresh_values, keys_pre, values_pre, segments):
    scale_factor = 1.0 / math.sqrt(HIDDEN_BREADTH // ASKING_CHANNELS)
    length = segments.shape[0]
    prefix_owner = jnp.arange(keys_pre.shape[1], dtype=jnp.int32) // (PPR * PAGE)
    mask_pre = (prefix_owner[None, :] == segments[:, None])[None]
    ordinal = jnp.arange(length, dtype=jnp.int32)
    mask_new = ((segments[None, :] == segments[:, None]) & (ordinal[None, :] <= ordinal[:, None]))[
        None
    ]
    scores_pre = (
        jnp.einsum("thd,hjd->htj", query_rows, keys_pre, preferred_element_type=jnp.float32)
        * scale_factor
    )
    scores_new = (
        jnp.einsum("thd,uhd->htu", query_rows, keys_new, preferred_element_type=jnp.float32)
        * scale_factor
    )
    weight_pre = jnp.where(mask_pre, jnp.exp(capped(scores_pre)), 0.0)
    weight_new = jnp.where(mask_new, jnp.exp(capped(scores_new)), 0.0)
    totals = jnp.sum(weight_pre, axis=-1, keepdims=True) + jnp.sum(
        weight_new, axis=-1, keepdims=True
    )
    probs_pre = (weight_pre / totals).astype(jnp.bfloat16)
    probs_new = (weight_new / totals).astype(jnp.bfloat16)
    mixture = jnp.einsum("htj,hjd->thd", probs_pre, values_pre, preferred_element_type=jnp.float32)
    mixture = mixture + jnp.einsum(
        "htu,uhd->thd", probs_new, fresh_values, preferred_element_type=jnp.float32
    )
    return mixture.astype(jnp.bfloat16).reshape(length, -1)


def shards(
    residual_input,
    before_attention_gain,
    after_attention_gain,
    before_feedforward_gain,
    after_feedforward_gain,
    query_weight,
    key_value_weight,
    output_weight,
    gate_matrix,
    up_matrix,
    down_matrix,
    key_value_cache,
    projected_lowrank_left,
    projected_lowrank_right,
    result_lowrank_left,
    result_lowrank_right,
    token_request,
    lowrank_choice_by_prompt,
    adapter_position,
    request_pages,
):
    mp_index = lax.axis_index(MP_AXES)
    dp_index = lax.axis_index(DP_AXES)
    residual = residual_input.astype(jnp.float32)
    normed_rows = rms_scale(residual, before_attention_gain).astype(jnp.bfloat16)
    normalized_rows = gather_mp(normed_rows)
    prompt_ordinal = normalized_rows.shape[0]
    channel_window = query_weight.shape[1] // CHANNEL_LENGTH
    query_rows = jnp.dot(normalized_rows, query_weight, preferred_element_type=jnp.float32).reshape(
        prompt_ordinal, channel_window, CHANNEL_LENGTH
    )
    key_value_rows = jnp.dot(
        normalized_rows,
        key_value_weight.reshape(HIDDEN_BREADTH, 2 * channel_window * CHANNEL_LENGTH),
        preferred_element_type=jnp.float32,
    ).reshape(prompt_ordinal, 2, channel_window, CHANNEL_LENGTH)
    segments = token_request[0]
    request_ids = lowrank_choice_by_prompt[0]
    request_range = jnp.arange(SHARD_PROMPTS, dtype=jnp.int32)
    membership = segments[:, None] == request_range[None, :]
    adapter_range = jnp.arange(NUM_LOW_TERMS, dtype=jnp.int32)
    token_adapter = jnp.sum(jnp.where(membership, request_ids[None, :], 0), axis=1)
    token_adapter_slot = jnp.sum(
        jnp.where(token_adapter[:, None] == adapter_range[None, :], adapter_position[None, :], 0),
        axis=1,
    )
    seat_count = projected_lowrank_left.shape[0]
    local_seats = mp_index * seat_count + jnp.arange(seat_count, dtype=jnp.int32)
    seat_factors = jnp.einsum(
        "td,sdk->tsk", normalized_rows, projected_lowrank_left, preferred_element_type=jnp.float32
    )
    seat_here = token_adapter_slot[:, None] == local_seats[None, :]
    lowrank_source = jnp.sum(jnp.where(seat_here[:, :, None], seat_factors, 0.0), axis=1)
    lowrank_source = sum_mp(lowrank_source.astype(jnp.bfloat16))
    choice_mask_table = membership.astype(jnp.bfloat16)
    broadened_lines = (choice_mask_table[:, :, None] * lowrank_source[:, None, :]).reshape(
        prompt_ordinal, SHARD_PROMPTS * LOW_DIMENSION
    )
    raised_result_lines = projected_lowrank_right[request_ids].reshape(
        SHARD_PROMPTS * LOW_DIMENSION, 3 * channel_window * CHANNEL_LENGTH
    )
    adapter_query_key_value = jnp.dot(
        broadened_lines, raised_result_lines, preferred_element_type=jnp.float32
    ).reshape(prompt_ordinal, 3, channel_window, CHANNEL_LENGTH)
    token_positions = positions_of(segments)
    rotary_queries = apply_rotary(
        query_rows + adapter_query_key_value[:, 0], token_positions
    ).astype(jnp.bfloat16)
    rotary_keys = apply_rotary(
        key_value_rows[:, 0] + adapter_query_key_value[:, 1], token_positions
    ).astype(jnp.bfloat16)
    fresh_values = (key_value_rows[:, 1] + adapter_query_key_value[:, 2]).astype(jnp.bfloat16)
    kv_new = jnp.stack([rotary_keys, fresh_values], axis=1)
    own_pages = lax.dynamic_index_in_dim(request_pages, dp_index, 0, keepdims=False).reshape(
        SHARD_PROMPTS * PPR
    )
    whole_pool = lax.all_gather(key_value_cache, DP_AXES, axis=0, tiled=True)
    chosen = whole_pool[own_pages]
    keys_pre = jnp.transpose(chosen[:, 0], (1, 0, 2, 3)).reshape(
        channel_window, SHARD_PROMPTS * PPR * PAGE, CHANNEL_LENGTH
    )
    values_pre = jnp.transpose(chosen[:, 1], (1, 0, 2, 3)).reshape(
        channel_window, SHARD_PROMPTS * PPR * PAGE, CHANNEL_LENGTH
    )
    attended = attend_local(
        rotary_queries, rotary_keys, fresh_values, keys_pre, values_pre, segments
    )
    request_output_down = result_lowrank_left[request_ids]
    request_output_factors = jnp.einsum(
        "tc,rck->trk", attended, request_output_down, preferred_element_type=jnp.float32
    )
    output_adapter_piece = jnp.sum(
        jnp.where(membership[:, :, None], request_output_factors, 0.0), axis=1
    )
    result_lowrank_source = sum_mp(output_adapter_piece).astype(jnp.bfloat16)
    result_seat_lines = result_lowrank_right.shape[0]
    output_slots = mp_index * result_seat_lines + jnp.arange(result_seat_lines, dtype=jnp.int32)
    resident_here = (token_adapter_slot[:, None] == output_slots[None, :]).astype(jnp.bfloat16)
    broadened_result = (resident_here[:, :, None] * result_lowrank_source[:, None, :]).reshape(
        prompt_ordinal, result_seat_lines * LOW_DIMENSION
    )
    raised_window = result_lowrank_right.reshape(result_seat_lines * LOW_DIMENSION, HIDDEN_BREADTH)
    attn_sum = scatter_mp(
        (
            jnp.dot(attended, output_weight, preferred_element_type=jnp.float32)
            + jnp.dot(broadened_result, raised_window, preferred_element_type=jnp.float32)
        ).astype(jnp.bfloat16)
    ).astype(jnp.float32)
    after_attn = (residual + rms_scale(attn_sum, after_attention_gain)).astype(jnp.bfloat16)
    normed_ffw = rms_scale(after_attn.astype(jnp.float32), before_feedforward_gain).astype(
        jnp.bfloat16
    )
    piece = gather_mp(normed_ffw)
    gated = jnp.dot(piece, gate_matrix, preferred_element_type=jnp.float32)
    upward = jnp.dot(piece, up_matrix, preferred_element_type=jnp.float32)
    hidden = (jax.nn.gelu(gated, approximate=True) * upward).astype(jnp.bfloat16)
    ffw_sum = scatter_mp(
        jnp.dot(hidden, down_matrix, preferred_element_type=jnp.float32).astype(jnp.bfloat16)
    ).astype(jnp.float32)
    hidden_out = (
        after_attn.astype(jnp.float32) + rms_scale(ffw_sum, after_feedforward_gain)
    ).astype(jnp.bfloat16)
    return (hidden_out, kv_new)


def solution(mesh):
    fine_mesh = jax.sharding.Mesh(mesh.devices.reshape(2, 2, 4, 4, 2), DP_AXES + MP_AXES)
    return jax.shard_map(
        shards,
        mesh=fine_mesh,
        in_specs=(
            P(DP_AXES + MP_AXES, None),
            P(),
            P(),
            P(),
            P(),
            P(None, MP_AXES),
            P(None, None, MP_AXES, None),
            P(MP_AXES, None),
            P(None, MP_AXES),
            P(None, MP_AXES),
            P(MP_AXES, None),
            P(DP_AXES, None, MP_AXES, None, None),
            P(MP_AXES, None, None),
            P(None, None, None, MP_AXES, None),
            P(None, MP_AXES, None),
            P(MP_AXES, None, None),
            P(DP_AXES, None),
            P(DP_AXES, None),
            P(),
            P(),
        ),
        out_specs=(P(DP_AXES + MP_AXES, None), P(DP_AXES, None, MP_AXES, None)),
        check_vma=False,
    )
```

profile of v0, /device:TPU:1, one launch (start us, length us, event | category | flops | bytes accessed | tf_op | source)
XLA Modules:
  0.0 553.6 jit_solution(13675936725571163932)
XLA Ops:
  10.1 6.8 %all_gather.16 = bf16[32,4608]{1,0:T(8,128)(2,1)} all-gather(bf16[16,4608]{1,0:T(8,128)(2,1)S(1)} %fusion.33), channel_id=1, replica_groups=mesh['zh'=2,'c'=2,'x'=4,'y'=4,'zl'=2] {'zl'}, dimensions={0}, use_global_device_ids=true | all-gather | bytes 442368 | tf_op jit(solution)/shard_map/all_gather | solution.py:24
  18.4 2.1 gather_fusion.2
  20.5 1.7 gather_fusion.1
  23.1 2.3 copy.60
  25.4 2.5 copy.50
  31.4 8.7 %all-gather.4.cloned.1.call-done = bf16[256,2,1,16,128]{4,3,2,1,0:T(8,128)(2,1)} async-done(((bf16[64,2,1,16,128]{4,3,2,1,0:T(8,128)(2,1)}), bf16[256,2,1,16,128]{4,3,2,1,0:T(8,128)(2,1)}) %all-gather.4.cloned.1.call-update) | async-done | bytes 2097168 | tf_op jit(solution)/shard_map/all_gather | solution.py:180
  40.0 2.9 gather_fusion
  44.6 50.0 %all-gather.6.cloned.1.call-done = bf16[512,4608]{1,0:T(8,128)(2,1)} async-done(((bf16[32,4608]{1,0:T(8,128)(2,1)}), bf16[512,4608]{1,0:T(8,128)(2,1)}) %all-gather.6.cloned.1.call-update) | async-done | bytes 4718608 | tf_op jit(solution)/shard_map/all_gather | solution.py:24
  94.5 3.8 fusion.84
  98.4 6.8 %psum.28 = bf16[512,16]{0,1:T(8,128)(2,1)} all-reduce(bf16[512,16]{0,1:T(8,128)(2,1)S(1)} %select_reduce_fusion.2), channel_id=1, replica_groups=mesh['zh'=2,'c'=2,'x'=4,'y'=4,'zl'=2] {'zl'}, use_global_device_ids=true, to_apply=%region_4.5 | all-reduce | flops 8192 | bytes 32768 | tf_op jit(solution)/shard_map/psum | solution.py:36
  105.2 58.5 %psum.29 = bf16[512,16]{0,1:T(8,128)(2,1)S(1)} all-reduce(bf16[512,16]{0,1:T(8,128)(2,1)} %psum.28), channel_id=1, replica_groups=mesh['zh'=2,'c'=2,'x'=4,'y'=4,'zl'=2] {'x','y'}, use_global_device_ids=true, to_apply=%region_5.6 | all-reduce | flops 8192 | bytes 32768 | tf_op jit(solution)/shard_map/psum | solution.py:36
  165.8 3.9 fusion.19
  173.9 5.6 %psum.30 = f32[512,16]{0,1:T(8,128)S(1)} all-reduce(f32[512,16]{0,1:T(8,128)S(1)} %select_reduce_fusion), channel_id=1, replica_groups=mesh['zh'=2,'c'=2,'x'=4,'y'=4,'zl'=2] {'zl'}, use_global_device_ids=true, to_apply=%region_10.11 | all-reduce | flops 8192 | bytes 65536 | tf_op jit(solution)/shard_map/psum | solution.py:36
  179.5 55.6 %psum.31 = bf16[512,16]{0,1:T(8,128)(2,1)S(1)} all-reduce(f32[512,16]{0,1:T(8,128)S(1)} %psum.30), channel_id=1, replica_groups=mesh['zh'=2,'c'=2,'x'=4,'y'=4,'zl'=2] {'x','y'}, use_global_device_ids=true, to_apply=%region_11.12 | all-reduce | flops 8192 | bytes 49152 | tf_op jit(solution)/shard_map/psum | solution.py:36
  236.6 3.5 fusion
  240.2 105.5 %reduce-scatter.5.cloned.1.call-done = bf16[32,4608]{1,0:T(8,128)(2,1)} async-done(((bf16[512,4608]{1,0:T(8,128)(2,1)}), bf16[32,4608]{1,0:T(8,128)(2,1)}) %reduce-scatter.5.cloned.1.call-update) | async-done | bytes 294928 | tf_op jit(solution)/shard_map/reduce_scatter | solution.py:30
  345.8 17.8 %reduce-scatter.7.cloned.1.call-done = bf16[16,4608]{1,0:T(8,128)(2,1)} async-done(((bf16[32,4608]{1,0:T(8,128)(2,1)}), bf16[16,4608]{1,0:T(8,128)(2,1)}) %reduce-scatter.7.cloned.1.call-update) | async-done | bytes 147472 | tf_op jit(solution)/shard_map/reduce_scatter | solution.py:30
  365.9 5.3 all_gather.18
  371.5 55.4 %all-gather.8.cloned.1.call-done = bf16[512,4608]{1,0:T(8,128)(2,1)} async-done(((bf16[32,4608]{1,0:T(8,128)(2,1)}), bf16[512,4608]{1,0:T(8,128)(2,1)}) %all-gather.8.cloned.1.call-update) | async-done | bytes 4718608 | tf_op jit(solution)/shard_map/all_gather | solution.py:24
  427.0 7.4 %fusion.85 = f32[512,640]{1,0:T(8,128)S(1)} fusion(bf16[512,4608]{1,0:T(8,128)(2,1)} %all-gather.8.cloned.1.call-done, bf16[4608,640]{1,0:T(8,128)(2,1)} %param.28), kind=kOutput, calls=%fused_computation.141 | convolution fusion | flops 3019898880 | bytes 11927552 | tf_op jit(solution)/shard_map/dot_general | solution.py:217
  434.4 14.3 %convolution_convert_fusion = bf16[512,4608]{1,0:T(8,128)(2,1)} fusion(bf16[640,4608]{1,0:T(8,128)(2,1)} %param.30, bf16[512,4608]{1,0:T(8,128)(2,1)} %all-gather.8.cloned.1.call-done, bf16[4608,640]{1,0:T(8,128)(2,1)} %param.29, f32[512,640]{1,0:T(8,128)S(1)} %fusion.85), kind=kOutput, calls=%fused_computation.5 | convolution fusion | flops 6045433856 | bytes 22544384 | tf_op jit(solution)/shard_map/dot_general | solution.py:221
  448.8 77.2 %reduce-scatter.9.cloned.1.call-done = bf16[32,4608]{1,0:T(8,128)(2,1)} async-done(((bf16[512,4608]{1,0:T(8,128)(2,1)}), bf16[32,4608]{1,0:T(8,128)(2,1)}) %reduce-scatter.9.cloned.1.call-update) | async-done | bytes 294928 | tf_op jit(solution)/shard_map/reduce_scatter | solution.py:30
  526.9 17.1 %reduce-scatter.11.cloned.1.call-done = bf16[16,4608]{1,0:T(8,128)(2,1)} async-done(((bf16[32,4608]{1,0:T(8,128)(2,1)}), bf16[16,4608]{1,0:T(8,128)(2,1)}) %reduce-scatter.11.cloned.1.call-update) | async-done | bytes 147472 | tf_op jit(solution)/shard_map/reduce_scatter | solution.py:30
  545.1 1.7 fusion.38
  (109 shorter events, 22.6 us)
Async XLA Ops:
  7.2 229.4 %copy-start = (bf16[128,4608]{1,0:T(8,128)(2,1)S(1)}, bf16[128,4608]{1,0:T(8,128)(2,1)}, u32[]{:S(2)}) copy-start(bf16[128,4608]{1,0:T(8,128)(2,1)} %param.27) | copy-start | bytes 3538948
  7.2 32.9 %all-gather.4.cloned.1.call-start = ((), (), s32[]{:S(2)}) async-start(), calls=%async_computation.4 | async-start | bytes 2621440 | tf_op jit(solution)/shard_map/all_gather | solution.py:180
  7.9 86.6 %all-gather.6.cloned.1.call-start = ((), (), s32[]{:S(2)}) async-start(), calls=%async_computation.5 | async-start | bytes 5013504 | tf_op jit(solution)/shard_map/all_gather | solution.py:24
  16.8 328.9 %reduce-scatter.5.cloned.1.call-start = ((), (), s32[]{:S(2)}) async-start(), calls=%async_computation.6 | async-start | bytes 5013504 | tf_op jit(solution)/shard_map/reduce_scatter | solution.py:30
  23.1 6.1 %copy-start.9 = (s32[1,512]{1,0:T(1,128)S(1)}, s32[1,512]{1,0:T(1,128)}, u32[]{:S(2)}) copy-start(s32[1,512]{1,0:T(1,128)} %param.36) | copy-start | bytes 6148
  23.1 6.1 %copy-start.19 = (s32[1,8]{1,0:T(1,128)S(1)}, s32[1,8]{1,0:T(1,128)}, u32[]{:S(2)}) copy-start(s32[1,8]{1,0:T(1,128)} %param.37) | copy-start | bytes 100
  23.1 6.2 %copy-start.20 = (s32[64]{0:T(128)S(1)}, s32[64]{0:T(128)}, u32[]{:S(2)}) copy-start(s32[64]{0:T(128)} %param.38) | copy-start | bytes 772
  27.9 137.8 %copy-start.3 = (bf16[256,4608]{1,0:T(8,128)(2,1)S(1)}, bf16[256,4608]{1,0:T(8,128)(2,1)}, u32[]{:S(2)}) copy-start(bf16[256,4608]{1,0:T(8,128)(2,1)} %copy.50) | copy-start | bytes 7077892
  94.5 3.9 copy-start.17
  164.4 5.3 slice-start
  165.7 4.0 slice-start.1
  165.7 4.0 copy-start.5
  169.8 2.4 copy-start.8
  173.1 62.0 %copy-start.6 = (bf16[2,16,4608]{2,1,0:T(8,128)(2,1)S(1)}, bf16[2,16,4608]{2,1,0:T(8,128)(2,1)}, u32[]{:S(2)}) copy-start(bf16[2,16,4608]{2,1,0:T(8,128)(2,1)} %param.35) | copy-start | bytes 884740
  173.1 62.0 %copy-start.15 = (bf16[512,2]{0,1:T(2,128)(2,1)S(1)}, bf16[512,2]{0,1:T(2,128)(2,1)}, u32[]{:S(2)}) copy-start(bf16[512,2]{0,1:T(2,128)(2,1)} %get-tuple-element.14) | copy-start | bytes 6148
  240.1 124.5 %copy-start.4 = (bf16[16,4608]{1,0:T(8,128)(2,1)S(1)}, bf16[16,4608]{1,0:T(8,128)(2,1)}, u32[]{:S(2)}) copy-start(bf16[16,4608]{1,0:T(8,128)(2,1)} %param.20) | copy-start | bytes 442372
  240.1 124.5 %copy-start.11 = (f32[4608]{0:T(1024)S(1)}, f32[4608]{0:T(1024)}, u32[]{:S(2)}) copy-start(f32[4608]{0:T(1024)} %param.22) | copy-start | bytes 55300
  240.1 125.7 %copy-start.12 = (f32[4608]{0:T(1024)S(1)}, f32[4608]{0:T(1024)}, u32[]{:S(2)}) copy-start(f32[4608]{0:T(1024)} %param.23) | copy-start | bytes 55300
  240.2 123.4 %reduce-scatter.7.cloned.1.call-start = ((), (), s32[]{:S(2)}) async-start(), calls=%async_computation.7 | async-start | bytes 442368 | tf_op jit(solution)/shard_map/reduce_scatter | solution.py:30
  345.7 81.2 %all-gather.8.cloned.1.call-start = ((), (), s32[]{:S(2)}) async-start(), calls=%async_computation.8 | async-start | bytes 5013504 | tf_op jit(solution)/shard_map/all_gather | solution.py:24
  371.3 154.7 %reduce-scatter.9.cloned.1.call-start = ((), (), s32[]{:S(2)}) async-start(), calls=%async_computation.9 | async-start | bytes 5013504 | tf_op jit(solution)/shard_map/reduce_scatter | solution.py:30
  434.4 112.4 %copy-start.1 = (bf16[128,4608]{1,0:T(8,128)(2,1)S(1)}, bf16[128,4608]{1,0:T(8,128)(2,1)}, u32[]{:S(2)}) copy-start(bf16[128,4608]{1,0:T(8,128)(2,1)} %param.27) | copy-start | bytes 3538948
  448.7 96.3 %copy-start.13 = (f32[4608]{0:T(1024)S(1)}, f32[4608]{0:T(1024)}, u32[]{:S(2)}) copy-start(f32[4608]{0:T(1024)} %param.24) | copy-start | bytes 55300
  448.7 95.2 %reduce-scatter.11.cloned.1.call-start = ((), (), s32[]{:S(2)}) async-start(), calls=%async_computation.10 | async-start | bytes 442368 | tf_op jit(solution)/shard_map/reduce_scatter | solution.py:30
  (7 other events, 12.2 us)
Sparse Core Ops, SparseCore 0:
  9.7 30.3 all-gather.3
  42.2 52.2 all-gather.5
  240.3 105.3 reduce-scatter.4
  347.9 15.6 reduce-scatter.6
  371.4 55.4 all-gather.7
  448.9 77.0 reduce-scatter.8
  528.3 15.6 reduce-scatter.10
where the time goes:
time: 554 us
  waiting for transfers between devices  332 us (60%)
  blocking collectives  139 us (25%)
  matrix products  39 us (7%)
  local copies, waits for them, and re-layouts  15.9 us (3%)
  between operations  14.6 us (3%)
  other arithmetic  12.7 us (2%)
    reduce_scatter x4, waiting for transfers between devices, scatter_mp(): values = lax.psum_scatter(values, stage, scatter_dimension=0, tiled=True)  218 us
    psum x4, blocking collectives, sum_mp(): values = lax.psum(values, stage)  127 us
    all_gather x2, waiting for transfers between devices, gather_mp(): values = lax.all_gather(values, stage, axis=0, tiled=True)  105 us
    dot_general x1, matrix products, shards(): jnp.dot(hidden, down_matrix, preferred_element_type=jnp.float32)  14.3 us
    all_gather x2, blocking collectives, gather_mp(): values = lax.all_gather(values, stage, axis=0, tiled=True)  12.1 us
  transfers between devices with their start and end apart: 7, of which 7 were waited for; matrix products, arithmetic and copies ran while one was open for 4% of the time, Pallas kernels for 0%

commit v1 on v0

--- a/solution.py
+++ b/solution.py
@@ -33,7 +33,11 @@
 
 def sum_mp(values):
     for stage in MP_STAGES:
-        values = lax.psum(values, stage)
+
+        def read_patches_up(original):
+            return jnp.sum(lax.all_gather(original, axis_name=stage), 0)
+
+        values = read_patches_up(values)
     return values
 
 

time: 554 us -> 457 us (0.82)
  blocking collectives: 139 us -> 53.7 us
  waiting for transfers between devices: 332 us -> 317 us
    psum x4 -> x0, blocking collectives: 127 us -> none  [sum_mp(): values = lax.psum(values, stage)]
    all_gather x0 -> x4, blocking collectives: none -> 41.6 us  [read_patches_up(): return jnp.sum(lax.all_gather(original, axis_name=stage), 0)]
    reduce_scatter x4, waiting for transfers between devices: 218 us -> 202 us  [scatter_mp(): values = lax.psum_scatter(values, stage, scatter_dimension=0, tiled=True)]
  transfers between devices with their start and end apart: 7 -> 7, of which waited for: 7 -> 7; matrix products, arithmetic and copies ran while one was open for 4% -> 5% of each run, Pallas kernels for 0% -> 0%
where the time goes in v1:
time: 457 us; the launch traced here: 456 us
  waiting for transfers between devices  317 us (69%)
  blocking collectives  53.7 us (12%)
  matrix products  38.9 us (9%)
  local copies, waits for them, and re-layouts  17.7 us (4%)
  between operations  14.6 us (3%)
  other arithmetic  13.8 us (3%)
    reduce_scatter x4, waiting for transfers between devices, scatter_mp(): values = lax.psum_scatter(values, stage, scatter_dimension=0, tiled=True)  202 us
    all_gather x2, waiting for transfers between devices, gather_mp(): values = lax.all_gather(values, stage, axis=0, tiled=True)  105 us
    all_gather x4, blocking collectives, read_patches_up(): return jnp.sum(lax.all_gather(original, axis_name=stage), 0)  41.6 us
    dot_general x1, matrix products, shards(): jnp.dot(hidden, down_matrix, preferred_element_type=jnp.float32)  14.3 us
    all_gather x2, blocking collectives, gather_mp(): values = lax.all_gather(values, stage, axis=0, tiled=True)  12.1 us
  transfers between devices with their start and end apart: 7, of which 7 were waited for; matrix products, arithmetic and copies ran while one was open for 5% of the time, Pallas kernels for 0%

profile of v1, /device:TPU:1, one launch (start us, length us, event | category | flops | bytes accessed | tf_op | source)
XLA Modules:
  0.0 455.9 jit_solution(11044738963353640985)
XLA Ops:
  10.1 6.8 %all_gather.38 = bf16[32,4608]{1,0:T(8,128)(2,1)} all-gather(bf16[16,4608]{1,0:T(8,128)(2,1)S(1)} %fusion.33), channel_id=1, replica_groups=mesh['zh'=2,'c'=2,'x'=4,'y'=4,'zl'=2] {'zl'}, dimensions={0}, use_global_device_ids=true | all-gather | bytes 442368 | tf_op jit(solution)/shard_map/all_gather | solution.py:24
  18.4 2.1 gather_fusion.2
  20.5 1.7 gather_fusion.1
  23.1 2.3 copy.71
  25.4 2.5 copy.59
  31.3 8.7 %all-gather.8.cloned.1.call-done = bf16[256,2,1,16,128]{4,3,2,1,0:T(8,128)(2,1)} async-done(((bf16[64,2,1,16,128]{4,3,2,1,0:T(8,128)(2,1)}), bf16[256,2,1,16,128]{4,3,2,1,0:T(8,128)(2,1)}) %all-gather.8.cloned.1.call-update) | async-done | bytes 2097168 | tf_op jit(solution)/shard_map/all_gather | solution.py:184
  40.0 2.9 gather_fusion
  44.6 50.0 %all-gather.10.cloned.1.call-done = bf16[512,4608]{1,0:T(8,128)(2,1)} async-done(((bf16[32,4608]{1,0:T(8,128)(2,1)}), bf16[512,4608]{1,0:T(8,128)(2,1)}) %all-gather.10.cloned.1.call-update) | async-done | bytes 4718608 | tf_op jit(solution)/shard_map/all_gather | solution.py:24
  94.5 3.8 fusion.84
  98.4 3.4 all-gather
  104.0 17.9 %all-gather.1 = bf16[8192,16]{0,1:T(8,128)(2,1)S(1)} all-gather(bf16[512,16]{0,1:T(8,128)(2,1)S(1)} %reduce_sum.145), channel_id=3, replica_groups=mesh['zh'=2,'c'=2,'x'=4,'y'=4,'zl'=2] {'x','y'}, dimensions={0}, use_global_device_ids=true | all-gather | bytes 278528 | tf_op jit(solution)/shard_map/all_gather | solution.py:38
  124.2 3.9 fusion.19
  132.3 3.4 all-gather.2
  135.9 16.9 %all-gather.3 = f32[8192,16]{0,1:T(8,128)S(1)} all-gather(f32[512,16]{0,1:T(8,128)S(1)} %reduce_sum.151), channel_id=5, replica_groups=mesh['zh'=2,'c'=2,'x'=4,'y'=4,'zl'=2] {'x','y'}, dimensions={0}, use_global_device_ids=true | all-gather | bytes 557056 | tf_op jit(solution)/shard_map/all_gather | solution.py:38
  154.7 3.5 fusion
  158.3 89.7 %reduce-scatter.5.cloned.1.call-done = bf16[32,4608]{1,0:T(8,128)(2,1)} async-done(((bf16[512,4608]{1,0:T(8,128)(2,1)}), bf16[32,4608]{1,0:T(8,128)(2,1)}) %reduce-scatter.5.cloned.1.call-update) | async-done | bytes 294928 | tf_op jit(solution)/shard_map/reduce_scatter | solution.py:30
  248.0 17.8 %reduce-scatter.7.cloned.1.call-done = bf16[16,4608]{1,0:T(8,128)(2,1)} async-done(((bf16[32,4608]{1,0:T(8,128)(2,1)}), bf16[16,4608]{1,0:T(8,128)(2,1)}) %reduce-scatter.7.cloned.1.call-update) | async-done | bytes 147472 | tf_op jit(solution)/shard_map/reduce_scatter | solution.py:30
  268.2 5.3 %all_gather.47 = bf16[32,4608]{1,0:T(8,128)(2,1)} all-gather(bf16[16,4608]{1,0:T(8,128)(2,1)S(1)} %fusion.37), channel_id=1, replica_groups=mesh['zh'=2,'c'=2,'x'=4,'y'=4,'zl'=2] {'zl'}, dimensions={0}, use_global_device_ids=true | all-gather | bytes 442368 | tf_op jit(solution)/shard_map/all_gather | solution.py:24
  273.7 55.4 %all-gather.12.cloned.1.call-done = bf16[512,4608]{1,0:T(8,128)(2,1)} async-done(((bf16[32,4608]{1,0:T(8,128)(2,1)}), bf16[512,4608]{1,0:T(8,128)(2,1)}) %all-gather.12.cloned.1.call-update) | async-done | bytes 4718608 | tf_op jit(solution)/shard_map/all_gather | solution.py:24
  329.2 7.4 %fusion.85 = f32[512,640]{1,0:T(8,128)S(1)} fusion(bf16[512,4608]{1,0:T(8,128)(2,1)} %all-gather.12.cloned.1.call-done, bf16[4608,640]{1,0:T(8,128)(2,1)} %param.28), kind=kOutput, calls=%fused_computation.143 | convolution fusion | flops 3019898880 | bytes 11927552 | tf_op jit(solution)/shard_map/dot_general | solution.py:221
  336.6 14.3 %convolution_convert_fusion = bf16[512,4608]{1,0:T(8,128)(2,1)} fusion(bf16[640,4608]{1,0:T(8,128)(2,1)} %param.30, bf16[512,4608]{1,0:T(8,128)(2,1)} %all-gather.12.cloned.1.call-done, bf16[4608,640]{1,0:T(8,128)(2,1)} %param.29, f32[512,640]{1,0:T(8,128)S(1)} %fusion.85), kind=kOutput, calls=%fused_computation.5 | convolution fusion | flops 6045433856 | bytes 22544384 | tf_op jit(solution)/shard_map/dot_general | solution.py:225
  351.0 77.3 %reduce-scatter.9.cloned.1.call-done = bf16[32,4608]{1,0:T(8,128)(2,1)} async-done(((bf16[512,4608]{1,0:T(8,128)(2,1)}), bf16[32,4608]{1,0:T(8,128)(2,1)}) %reduce-scatter.9.cloned.1.call-update) | async-done | bytes 294928 | tf_op jit(solution)/shard_map/reduce_scatter | solution.py:30
  429.2 17.1 %reduce-scatter.11.cloned.1.call-done = bf16[16,4608]{1,0:T(8,128)(2,1)} async-done(((bf16[32,4608]{1,0:T(8,128)(2,1)}), bf16[16,4608]{1,0:T(8,128)(2,1)}) %reduce-scatter.11.cloned.1.call-update) | async-done | bytes 147472 | tf_op jit(solution)/shard_map/reduce_scatter | solution.py:30
  447.4 1.7 fusion.38
  (115 shorter events, 25.5 us)
Async XLA Ops:
  7.2 147.5 %copy-start = (bf16[128,4608]{1,0:T(8,128)(2,1)S(1)}, bf16[128,4608]{1,0:T(8,128)(2,1)}, u32[]{:S(2)}) copy-start(bf16[128,4608]{1,0:T(8,128)(2,1)} %param.27) | copy-start | bytes 3538948
  7.2 32.9 %all-gather.8.cloned.1.call-start = ((), (), s32[]{:S(2)}) async-start(), calls=%async_computation.4 | async-start | bytes 2621440 | tf_op jit(solution)/shard_map/all_gather | solution.py:184
  7.9 86.6 %all-gather.10.cloned.1.call-start = ((), (), s32[]{:S(2)}) async-start(), calls=%async_computation.5 | async-start | bytes 5013504 | tf_op jit(solution)/shard_map/all_gather | solution.py:24
  16.8 231.1 %reduce-scatter.5.cloned.1.call-start = ((), (), s32[]{:S(2)}) async-start(), calls=%async_computation.6 | async-start | bytes 5013504 | tf_op jit(solution)/shard_map/reduce_scatter | solution.py:30
  23.1 6.0 %copy-start.9 = (s32[1,512]{1,0:T(1,128)S(1)}, s32[1,512]{1,0:T(1,128)}, u32[]{:S(2)}) copy-start(s32[1,512]{1,0:T(1,128)} %param.36) | copy-start | bytes 6148
  23.1 6.0 %copy-start.18 = (s32[1,8]{1,0:T(1,128)S(1)}, s32[1,8]{1,0:T(1,128)}, u32[]{:S(2)}) copy-start(s32[1,8]{1,0:T(1,128)} %param.37) | copy-start | bytes 100
  23.1 6.1 %copy-start.19 = (s32[64]{0:T(128)S(1)}, s32[64]{0:T(128)}, u32[]{:S(2)}) copy-start(s32[64]{0:T(128)} %param.38) | copy-start | bytes 772
  27.9 96.2 %copy-start.3 = (bf16[256,4608]{1,0:T(8,128)(2,1)S(1)}, bf16[256,4608]{1,0:T(8,128)(2,1)}, u32[]{:S(2)}) copy-start(bf16[256,4608]{1,0:T(8,128)(2,1)} %copy.59) | copy-start | bytes 7077892
  122.8 5.3 %slice-start = ((s8[4718592]{0:T(1024)(128)(4,1)}), s8[4194304]{0:T(1024)(128)(4,1)S(1)}, s32[]{:S(2)}) async-start(s8[4718592]{0:T(1024)(128)(4,1)} %bitcast.114), calls=%async_computation.11 | async-start | bytes 8388608
  124.1 4.0 slice-start.1
  124.1 4.0 copy-start.5
  128.2 2.4 copy-start.8
  128.2 2.4 copy-start.10
  131.6 21.7 %copy-start.6 = (bf16[2,16,4608]{2,1,0:T(8,128)(2,1)S(1)}, bf16[2,16,4608]{2,1,0:T(8,128)(2,1)}, u32[]{:S(2)}) copy-start(bf16[2,16,4608]{2,1,0:T(8,128)(2,1)} %param.35) | copy-start | bytes 884740
  131.6 21.7 %copy-start.15 = (bf16[512,2]{0,1:T(2,128)(2,1)S(1)}, bf16[512,2]{0,1:T(2,128)(2,1)}, u32[]{:S(2)}) copy-start(bf16[512,2]{0,1:T(2,128)(2,1)} %get-tuple-element.16) | copy-start | bytes 6148
  158.2 108.7 %copy-start.4 = (bf16[16,4608]{1,0:T(8,128)(2,1)S(1)}, bf16[16,4608]{1,0:T(8,128)(2,1)}, u32[]{:S(2)}) copy-start(bf16[16,4608]{1,0:T(8,128)(2,1)} %param.20) | copy-start | bytes 442372
  158.2 108.7 %copy-start.11 = (f32[4608]{0:T(1024)S(1)}, f32[4608]{0:T(1024)}, u32[]{:S(2)}) copy-start(f32[4608]{0:T(1024)} %param.22) | copy-start | bytes 55300
  158.2 109.9 %copy-start.12 = (f32[4608]{0:T(1024)S(1)}, f32[4608]{0:T(1024)}, u32[]{:S(2)}) copy-start(f32[4608]{0:T(1024)} %param.23) | copy-start | bytes 55300
  158.2 107.6 %reduce-scatter.7.cloned.1.call-start = ((), (), s32[]{:S(2)}) async-start(), calls=%async_computation.7 | async-start | bytes 442368 | tf_op jit(solution)/shard_map/reduce_scatter | solution.py:30
  248.0 81.2 %all-gather.12.cloned.1.call-start = ((), (), s32[]{:S(2)}) async-start(), calls=%async_computation.8 | async-start | bytes 5013504 | tf_op jit(solution)/shard_map/all_gather | solution.py:24
  273.5 154.8 %reduce-scatter.9.cloned.1.call-start = ((), (), s32[]{:S(2)}) async-start(), calls=%async_computation.9 | async-start | bytes 5013504 | tf_op jit(solution)/shard_map/reduce_scatter | solution.py:30
  336.6 112.5 %copy-start.1 = (bf16[128,4608]{1,0:T(8,128)(2,1)S(1)}, bf16[128,4608]{1,0:T(8,128)(2,1)}, u32[]{:S(2)}) copy-start(bf16[128,4608]{1,0:T(8,128)(2,1)} %param.27) | copy-start | bytes 3538948
  350.9 96.5 %copy-start.13 = (f32[4608]{0:T(1024)S(1)}, f32[4608]{0:T(1024)}, u32[]{:S(2)}) copy-start(f32[4608]{0:T(1024)} %param.24) | copy-start | bytes 55300
  350.9 95.4 %reduce-scatter.11.cloned.1.call-start = ((), (), s32[]{:S(2)}) async-start(), calls=%async_computation.10 | async-start | bytes 442368 | tf_op jit(solution)/shard_map/reduce_scatter | solution.py:30
  (6 other events, 9.8 us)
Sparse Core Ops, SparseCore 0:
  9.7 30.3 all-gather.7
  42.2 52.2 all-gather.9
  158.3 89.5 reduce-scatter.4
  250.1 15.5 reduce-scatter.6
  273.6 55.4 all-gather.11
  351.1 77.1 reduce-scatter.8
  430.6 15.6 reduce-scatter.10
